TPU v7x, 32 devices: a whole 2x2x4 slice. The times are simulated.
32 devices in a mesh: batch: 4 (over z), seq: 8 (over y, x, core).
Axes of the slice: x: 2, y: 2, z: 4, core: 2. Of those that a mesh axis runs over, the one named last changes fastest.
Arguments:
- block_input: bfloat16 [16384, 768], P(('batch', 'seq')), may hold values from -6 to 6
- history: bfloat16 [8, 16384, 768], P(None, ('batch', 'seq')), may hold values from -6 to 6
- cotangent: bfloat16 [16384, 768], P(('batch', 'seq')), may hold values from -6 to 6
- qkv_weight: bfloat16 [768, 2304], P('batch', 'seq'), may hold values from -0.21875 to 0.21875
- proj_weight: bfloat16 [768, 768], P('batch', 'seq'), may hold values from -1.25 to 1.25
- up_weight: bfloat16 [768, 3072], P('batch', 'seq'), may hold values from -0.21875 to 0.21875
- down_weight: bfloat16 [3072, 768], P('batch', 'seq'), may hold values from -0.109375 to 0.109375
- norm1_gain: float32 [768], replicated, may hold values from 0.5 to 1.5
- norm1_bias: float32 [768], replicated, may hold values from -1.2 to 1.2
- norm2_gain: float32 [768], replicated, may hold values from 0.5 to 1.5
- norm2_bias: float32 [768], replicated, may hold values from -1.2 to 1.2
- dwa_weights: float32 [9], replicated, may hold values from 0.3 to 1
- pair_order: int32 [4, 24], P('batch'), may hold values from 0 to 23, each once within a row
- long_group: int32 [4, 2], P('batch'), may hold values from 0 to 2
Outputs:
- block_output: bfloat16 [16384, 768], P(('batch', 'seq'))
- input_grad: bfloat16 [16384, 768], P(('batch', 'seq'))
- history_grad: bfloat16 [8, 16384, 768], P(None, ('batch', 'seq'))
- row_lse: float32 [4, 24, 2048], P('batch', 'seq')
- qkv_grad: float32 [768, 2304], P('batch', 'seq')
- proj_grad: float32 [768, 768], P('batch', 'seq')
- up_grad: float32 [768, 3072], P('batch', 'seq')
- down_grad: float32 [3072, 768], P('batch', 'seq')
- norm1_gain_grad: float32 [768], replicated
- norm1_bias_grad: float32 [768], replicated
- norm2_gain_grad: float32 [768], replicated
- norm2_bias_grad: float32 [768], replicated
- dwa_grad: float32 [9], replicated
Inputs may be any that keep to these rules, and one draw needn't show every extreme that they name: `pair_order`: each row lists each of its group's 24 pairs once. `long_group`: an entry v: that slot holds 2^v sequences of 2048 // 2^v tokens.
All inputs are finite; a program needn't handle non-finite values.
Results may differ from a plain program's by a relative error of at most 0.017.
Values may be sent and summed in bfloat16 or wider, within the bound.
No kernel may reach another device: no remote copies, remote signals or barrier semaphores. Data moves between devices by JAX's collectives and lax.ppermute only.
A program may use at most 192 MiB of HBM per device.

v0:
```python
import jax
import jax.numpy as jnp
from jax import lax
from jax.sharding import PartitionSpec as P

D = 768
HEADS = 12
HD = 64
SLOT = 2048
HIST = 8
NORM_EPS = 1e-05
MASKED = -1e30


def norm_rows(values, gain, shift):
    row_mean = jnp.mean(values, axis=-1, keepdims=True)
    centred = values - row_mean
    variance = jnp.mean(centred * centred, axis=-1, keepdims=True)
    inv_std = lax.rsqrt(variance + NORM_EPS)
    normed = centred * inv_std
    return (normed * gain + shift, normed, inv_std)


def norm_back(grad_in, normed, inv_std, gain):
    scaled = grad_in * gain
    centred = (
        scaled
        - jnp.mean(scaled, axis=-1, keepdims=True)
        - normed * jnp.mean(scaled * normed, axis=-1, keepdims=True)
    )
    return (centred * inv_std, jnp.sum(grad_in * normed, axis=0), jnp.sum(grad_in, axis=0))


def rotate(values, cosine, sine_tab):
    half_size = values.shape[-1] // 2
    front = values[..., :half_size]
    behind = values[..., half_size:]
    cos_part = cosine[..., None, :]
    sin_part = sine_tab[..., None, :]
    return jnp.concatenate(
        [front * cos_part - behind * sin_part, behind * cos_part + front * sin_part], axis=-1
    )


def unrotate(values, cosine, sine_tab):
    half_size = values.shape[-1] // 2
    front = values[..., :half_size]
    behind = values[..., half_size:]
    cos_part = cosine[..., None, :]
    sin_part = sine_tab[..., None, :]
    return jnp.concatenate(
        [front * cos_part + behind * sin_part, behind * cos_part - front * sin_part], axis=-1
    )


def to_pairs(stacked, order_row, n_seq, per_dev):
    slot_count, piece_len, part_count, head_count, head_size = stacked.shape
    reordered = jnp.transpose(stacked, (0, 3, 2, 1, 4)).reshape(
        slot_count * head_count, part_count, piece_len * head_size
    )
    return jnp.take(reordered, order_row, axis=0).reshape(
        n_seq, per_dev, part_count, piece_len * head_size
    )


def pairs_whole(incoming, head_size):
    n_seq, per_dev, part_count, flat_len = incoming.shape
    piece_len = flat_len // head_size
    reordered = jnp.transpose(
        incoming.reshape(n_seq, per_dev, part_count, piece_len, head_size), (1, 2, 0, 3, 4)
    )
    return reordered.reshape(per_dev, part_count, n_seq * piece_len, head_size)


def pairs_split(whole_seq, n_seq):
    per_dev, part_count, seq_len, head_size = whole_seq.shape
    return jnp.transpose(
        whole_seq.reshape(per_dev, part_count, n_seq, seq_len // n_seq * head_size), (2, 0, 1, 3)
    )


def tokens_back(incoming, inverse, slot_count, head_size):
    n_seq, per_dev, part_count, flat_len = incoming.shape
    piece_len = flat_len // head_size
    ordered = jnp.take(incoming.reshape(n_seq * per_dev, part_count, flat_len), inverse, axis=0)
    head_count = n_seq * per_dev // slot_count
    return jnp.transpose(
        ordered.reshape(slot_count, head_count, part_count, piece_len, head_size), (0, 3, 2, 1, 4)
    )


def local(
    block_input,
    history,
    cotangent,
    qkv_weight,
    proj_weight,
    up_weight,
    down_weight,
    norm1_gain,
    norm1_bias,
    norm2_gain,
    norm2_bias,
    dwa_weights,
    pair_order,
    long_group,
):
    n_seq = lax.axis_size("seq")
    row_count = block_input.shape[0]
    piece_len = SLOT // n_seq
    slot_count = row_count // piece_len
    pair_count = slot_count * HEADS
    per_dev = pair_count // n_seq
    block_rows = min(512, SLOT)
    block_count = SLOT // block_rows
    score_scale = HD ** (-0.5)
    slot_flags = long_group[0]
    seg_len = SLOT // jnp.left_shift(jnp.ones_like(slot_flags), slot_flags)
    position = jnp.arange(SLOT, dtype=jnp.int32)
    segment_all = position[None, :] // seg_len[:, None]
    doc_place = (position[None, :] % seg_len[:, None]).astype(jnp.float32)
    frequency = jnp.power(10000.0, jnp.arange(HD // 2, dtype=jnp.float32) * (-2.0 / HD))
    angles = doc_place[..., None] * frequency
    my_index = lax.axis_index("seq")
    my_start = my_index * piece_len
    cosine = lax.dynamic_slice_in_dim(jnp.cos(angles), my_start, piece_len, 1)
    sine_tab = lax.dynamic_slice_in_dim(jnp.sin(angles), my_start, piece_len, 1)
    order_row = pair_order[0]
    inverse = (
        jnp.zeros((pair_count,), jnp.int32)
        .at[order_row]
        .set(jnp.arange(pair_count, dtype=jnp.int32))
    )
    held_pairs = lax.dynamic_slice_in_dim(order_row, my_index * per_dev, per_dev, 0)
    pair_segment = jnp.take(segment_all, held_pairs // HEADS, axis=0)
    row_parts = (
        lax.all_gather(qkv_weight, "batch", axis=0, tiled=True),
        lax.all_gather(proj_weight, "batch", axis=0, tiled=True),
        lax.all_gather(up_weight, "batch", axis=0, tiled=True),
        lax.all_gather(down_weight, "batch", axis=0, tiled=True),
    )
    w_qkv, w_proj, w_up, w_down = (
        lax.all_gather(row_parts[0], "seq", axis=1, tiled=True),
        lax.all_gather(row_parts[1], "seq", axis=1, tiled=True),
        lax.all_gather(row_parts[2], "seq", axis=1, tiled=True),
        lax.all_gather(row_parts[3], "seq", axis=1, tiled=True),
    )
    inputs32 = block_input.astype(jnp.float32)
    norm1_out, normed1, inv_std1 = norm_rows(inputs32, norm1_gain, norm1_bias)
    norm1_low = norm1_out.astype(jnp.bfloat16)
    qkv_out = jnp.dot(norm1_low, w_qkv, preferred_element_type=jnp.float32)
    queries = rotate(qkv_out[:, :D].reshape(slot_count, piece_len, HEADS, HD), cosine, sine_tab)
    keys_rot = rotate(
        qkv_out[:, D : 2 * D].reshape(slot_count, piece_len, HEADS, HD), cosine, sine_tab
    )
    values_in = qkv_out[:, 2 * D :].reshape(slot_count, piece_len, HEADS, HD)
    stacked = jnp.stack([queries, keys_rot, values_in], axis=2).astype(jnp.bfloat16)
    incoming = lax.all_to_all(
        to_pairs(stacked, order_row, n_seq, per_dev), "seq", split_axis=0, concat_axis=0, tiled=True
    )
    sequences = pairs_whole(incoming, HD)
    query_pairs = sequences[:, 0]
    key_pairs = sequences[:, 1]
    value_pairs = sequences[:, 2]

    def masked_scores(start_row, query_block):
        raw_scores = jnp.einsum(
            "pqd,pkd->pqk", query_block, key_pairs, preferred_element_type=jnp.float32
        )
        query_place = start_row + jnp.arange(block_rows, dtype=jnp.int32)
        query_seg = lax.dynamic_slice_in_dim(pair_segment, start_row, block_rows, 1)
        allowed = (position[None, None, :] <= query_place[None, :, None]) & (
            pair_segment[:, None, :] == query_seg[:, :, None]
        )
        return jnp.where(allowed, raw_scores * score_scale, MASKED)

    def forward_block(start_row):
        query_block = lax.dynamic_slice_in_dim(query_pairs, start_row, block_rows, 1)
        scores = masked_scores(start_row, query_block)
        row_top = jnp.max(scores, axis=-1, keepdims=True)
        weights_exp = jnp.exp(scores - row_top)
        row_total = jnp.sum(weights_exp, axis=-1, keepdims=True)
        probability = (weights_exp / row_total).astype(jnp.bfloat16)
        attn_block = jnp.einsum(
            "pqk,pkd->pqd", probability, value_pairs, preferred_element_type=jnp.float32
        ).astype(jnp.bfloat16)
        return (attn_block, row_top[..., 0] + jnp.log(row_total[..., 0]))

    starts = jnp.arange(block_count, dtype=jnp.int32) * block_rows
    attn_blocks, totals = lax.map(forward_block, starts)
    attended_pairs = jnp.transpose(attn_blocks, (1, 0, 2, 3)).reshape(per_dev, 1, SLOT, HD)
    log_total = jnp.transpose(totals, (1, 0, 2)).reshape(per_dev, SLOT)
    returned = lax.all_to_all(
        pairs_split(attended_pairs, n_seq), "seq", split_axis=0, concat_axis=0, tiled=True
    )
    attended = tokens_back(returned, inverse, slot_count, HD).reshape(row_count, D)
    middle = inputs32 + jnp.dot(attended, w_proj, preferred_element_type=jnp.float32)
    norm2_out, normed2, inv_std2 = norm_rows(middle, norm2_gain, norm2_bias)
    norm2_low = norm2_out.astype(jnp.bfloat16)
    hidden_up = jnp.dot(norm2_low, w_up, preferred_element_type=jnp.float32)
    gelu_out, gelu_pull = jax.vjp(lambda hidden: jax.nn.gelu(hidden, approximate=True), hidden_up)
    gelu_low = gelu_out.astype(jnp.bfloat16)
    block_out = middle + jnp.dot(gelu_low, w_down, preferred_element_type=jnp.float32)
    dwa_out = dwa_weights[HIST] * block_out
    for layer_idx in range(HIST):
        dwa_out = dwa_out + dwa_weights[layer_idx] * history[layer_idx].astype(jnp.float32)
    block_output = dwa_out.astype(jnp.bfloat16)
    grad_out = cotangent.astype(jnp.float32)
    history_grad = (dwa_weights[:HIST, None, None] * grad_out[None]).astype(jnp.bfloat16)
    dwa_terms = [
        jnp.sum(history[layer_idx].astype(jnp.float32) * grad_out) for layer_idx in range(HIST)
    ]
    dwa_terms.append(jnp.sum(block_out * grad_out))
    dwa_local = jnp.stack(dwa_terms)
    again_parts = (
        lax.all_gather(qkv_weight, "batch", axis=0, tiled=True),
        lax.all_gather(proj_weight, "batch", axis=0, tiled=True),
        lax.all_gather(up_weight, "batch", axis=0, tiled=True),
        lax.all_gather(down_weight, "batch", axis=0, tiled=True),
    )
    w_qkv, w_proj, w_up, w_down = (
        lax.all_gather(again_parts[0], "seq", axis=1, tiled=True),
        lax.all_gather(again_parts[1], "seq", axis=1, tiled=True),
        lax.all_gather(again_parts[2], "seq", axis=1, tiled=True),
        lax.all_gather(again_parts[3], "seq", axis=1, tiled=True),
    )
    dy_full = dwa_weights[HIST] * grad_out
    dmlp_low = dy_full.astype(jnp.bfloat16)
    down_local = jnp.einsum("nf,nd->fd", gelu_low, dmlp_low, preferred_element_type=jnp.float32)
    dgelu = jnp.einsum("nd,fd->nf", dmlp_low, w_down, preferred_element_type=jnp.float32)
    dup_low = gelu_pull(dgelu)[0].astype(jnp.bfloat16)
    up_local = jnp.einsum("nd,nf->df", norm2_low, dup_low, preferred_element_type=jnp.float32)
    dnorm2 = jnp.einsum("nf,df->nd", dup_low, w_up, preferred_element_type=jnp.float32)
    dmid_norm, gain2_local, bias2_local = norm_back(dnorm2, normed2, inv_std2, norm2_gain)
    dmiddle = dy_full + dmid_norm
    dmiddle_low = dmiddle.astype(jnp.bfloat16)
    proj_local = jnp.einsum("nd,ne->de", attended, dmiddle_low, preferred_element_type=jnp.float32)
    dattended = jnp.einsum(
        "ne,de->nd", dmiddle_low, w_proj, preferred_element_type=jnp.float32
    ).astype(jnp.bfloat16)
    dattn_tokens = dattended.reshape(slot_count, piece_len, 1, HEADS, HD)
    dattn_in = lax.all_to_all(
        to_pairs(dattn_tokens, order_row, n_seq, per_dev),
        "seq",
        split_axis=0,
        concat_axis=0,
        tiled=True,
    )
    dout_pairs = pairs_whole(dattn_in, HD)[:, 0]

    def backward_block(sums_carry, start_row):
        dkeys_sum, dvalues_sum = sums_carry
        query_block = lax.dynamic_slice_in_dim(query_pairs, start_row, block_rows, 1)
        dout_block = lax.dynamic_slice_in_dim(dout_pairs, start_row, block_rows, 1)
        total_block = lax.dynamic_slice_in_dim(log_total, start_row, block_rows, 1)
        probability = jnp.exp(masked_scores(start_row, query_block) - total_block[..., None])
        prob_low = probability.astype(jnp.bfloat16)
        dprob_full = jnp.einsum(
            "pqd,pkd->pqk", dout_block, value_pairs, preferred_element_type=jnp.float32
        )
        row_delta = jnp.sum(probability * dprob_full, axis=-1, keepdims=True)
        dscore = (probability * (dprob_full - row_delta) * score_scale).astype(jnp.bfloat16)
        dquery_block = jnp.einsum(
            "pqk,pkd->pqd", dscore, key_pairs, preferred_element_type=jnp.float32
        )
        dkeys_sum = dkeys_sum + jnp.einsum(
            "pqk,pqd->pkd", dscore, query_block, preferred_element_type=jnp.float32
        )
        dvalues_sum = dvalues_sum + jnp.einsum(
            "pqk,pqd->pkd", prob_low, dout_block, preferred_element_type=jnp.float32
        )
        return ((dkeys_sum, dvalues_sum), dquery_block)

    zero_pairs = jnp.zeros((per_dev, SLOT, HD), jnp.float32)
    (dkeys_sum, dvalues_sum), dquery_blocks = lax.scan(
        backward_block, (zero_pairs, zero_pairs), starts
    )
    dquery = jnp.transpose(dquery_blocks, (1, 0, 2, 3)).reshape(per_dev, SLOT, HD)
    dpairs = jnp.stack([dquery, dkeys_sum, dvalues_sum], axis=1).astype(jnp.bfloat16)
    dreturned = lax.all_to_all(
        pairs_split(dpairs, n_seq), "seq", split_axis=0, concat_axis=0, tiled=True
    )
    dtokens = tokens_back(dreturned, inverse, slot_count, HD)
    dq_rows = unrotate(dtokens[:, :, 0].astype(jnp.float32), cosine, sine_tab).reshape(row_count, D)
    dk_rows = unrotate(dtokens[:, :, 1].astype(jnp.float32), cosine, sine_tab).reshape(row_count, D)
    dv_rows = dtokens[:, :, 2].astype(jnp.float32).reshape(row_count, D)
    dqkv_low = jnp.concatenate([dq_rows, dk_rows, dv_rows], axis=-1).astype(jnp.bfloat16)
    qkv_local = jnp.einsum("nd,nf->df", norm1_low, dqkv_low, preferred_element_type=jnp.float32)
    dnorm1 = jnp.einsum("nf,df->nd", dqkv_low, w_qkv, preferred_element_type=jnp.float32)
    dinput_norm, gain1_local, bias1_local = norm_back(dnorm1, normed1, inv_std1, norm1_gain)
    input_grad = (dmiddle + dinput_norm).astype(jnp.bfloat16)
    col_sums = (
        lax.psum_scatter(
            qkv_local.astype(jnp.bfloat16), "seq", scatter_dimension=1, tiled=True
        ).astype(jnp.float32),
        lax.psum_scatter(
            proj_local.astype(jnp.bfloat16), "seq", scatter_dimension=1, tiled=True
        ).astype(jnp.float32),
        lax.psum_scatter(
            up_local.astype(jnp.bfloat16), "seq", scatter_dimension=1, tiled=True
        ).astype(jnp.float32),
        lax.psum_scatter(
            down_local.astype(jnp.bfloat16), "seq", scatter_dimension=1, tiled=True
        ).astype(jnp.float32),
    )
    qkv_grad, proj_grad, up_grad, down_grad = (
        lax.psum_scatter(
            col_sums[0].astype(jnp.bfloat16), "batch", scatter_dimension=0, tiled=True
        ).astype(jnp.float32),
        lax.psum_scatter(
            col_sums[1].astype(jnp.bfloat16), "batch", scatter_dimension=0, tiled=True
        ).astype(jnp.float32),
        lax.psum_scatter(
            col_sums[2].astype(jnp.bfloat16), "batch", scatter_dimension=0, tiled=True
        ).astype(jnp.float32),
        lax.psum_scatter(
            col_sums[3].astype(jnp.bfloat16), "batch", scatter_dimension=0, tiled=True
        ).astype(jnp.float32),
    )
    gain1_grad, bias1_grad, gain2_grad, bias2_grad, dwa_grad = lax.psum(
        (gain1_local, bias1_local, gain2_local, bias2_local, dwa_local), ("batch", "seq")
    )
    row_lse = log_total.reshape(1, per_dev, SLOT)
    return (
        block_output,
        input_grad,
        history_grad,
        row_lse,
        qkv_grad,
        proj_grad,
        up_grad,
        down_grad,
        gain1_grad,
        bias1_grad,
        gain2_grad,
        bias2_grad,
        dwa_grad,
    )


def solution(mesh):
    placed = (
        P(("batch", "seq"), None),
        P(None, ("batch", "seq"), None),
        P(("batch", "seq"), None),
        P("batch", "seq"),
        P("batch", "seq"),
        P("batch", "seq"),
        P("batch", "seq"),
        P(),
        P(),
        P(),
        P(),
        P(),
        P("batch", None),
        P("batch", None),
    )
    return jax.shard_map(
        local,
        mesh=mesh,
        in_specs=placed,
        out_specs=(
            P(("batch", "seq"), None),
            P(("batch", "seq"), None),
            P(None, ("batch", "seq"), None),
            P("batch", "seq", None),
            P("batch", "seq"),
            P("batch", "seq"),
            P("batch", "seq"),
            P("batch", "seq"),
            P(),
            P(),
            P(),
            P(),
            P(),
        ),
        check_vma=False,
    )
```

profile of v0, /device:TPU:0, one launch (start us, length us, event | category | flops | bytes accessed | tf_op | source)
XLA Modules:
  0.0 866.0 jit_solution(16337869639670817424)
XLA Ops:
  7.3 18.6 %all_gather.32 = bf16[768,288]{1,0:T(8,128)(2,1)S(1)} all-gather(bf16[192,288]{1,0:T(8,128)(2,1)} %param.25), channel_id=1, replica_groups=mesh['batch'=4,'seq'=8] {'batch'}, dimensions={0}, use_global_device_ids=true | all-gather | bytes 552960 | tf_op jit(solution)/shard_map/all_gather | solution.py:137
  27.0 13.8 %all_gather.34 = bf16[768,96]{1,0:T(8,128)(2,1)S(1)} all-gather(bf16[192,96]{1,0:T(8,128)(2,1)} %param.26), channel_id=1, replica_groups=mesh['batch'=4,'seq'=8] {'batch'}, dimensions={0}, use_global_device_ids=true | all-gather | bytes 184320 | tf_op jit(solution)/shard_map/all_gather | solution.py:138
  41.7 17.0 %all_gather.36 = bf16[768,384]{1,0:T(8,128)(2,1)} all-gather(bf16[192,384]{1,0:T(8,128)(2,1)S(1)} %copy-done.18), channel_id=1, replica_groups=mesh['batch'=4,'seq'=8] {'batch'}, dimensions={0}, use_global_device_ids=true | all-gather | bytes 737280 | tf_op jit(solution)/shard_map/all_gather | solution.py:139
  91.2 8.2 reshape.607
  99.4 7.2 gather_fusion.1
  116.1 17.4 %all_gather.38 = bf16[3072,96]{0,1:T(8,128)(2,1)} all-gather(bf16[768,96]{0,1:T(8,128)(2,1)S(1)} %copy-done.19), channel_id=1, replica_groups=mesh['batch'=4,'seq'=8] {'batch'}, dimensions={0}, use_global_device_ids=true | all-gather | bytes 737280 | tf_op jit(solution)/shard_map/all_gather | solution.py:140
  134.2 27.8 %all-to-all-done = bf16[8,3,3,16384]{3,1,2,0:T(4,128)(2,1)S(1)} async-done(((bf16[8,3,3,16384]{3,1,2,0:T(4,128)(2,1)}), bf16[8,3,3,16384]{3,1,2,0:T(4,128)(2,1)S(1)}, u32[]{:S(2)}, u32[]{:S(2)}) %all-to-all-start) | async-done | bytes 2359328 | tf_op jit(solution)/shard_map/all_to_all | solution.py:158
  165.2 7.1 reshape.515
  181.9 80.8 %while.28 = (s32[]{:T(128)}, bf16[4,3,512,64]{2,3,1,0:T(8,128)(2,1)}, f32[4,3,512]{2,1,0:T(4,128)S(1)}, s32[4]{0:T(128)S(1)}, s32[3,2048]{1,0:T(4,128)S(1)}, /*i...) while((s32[]{:T(128)}, ...), condition=%wide.region_5.7_spmd.clone, body=%wide.region_2.6_spmd.clone.sunk | while | flops 863075328 | bytes 44073140 | solution.py:190
  185.8 5.5 fusion.157
  196.3 5.8 fusion.159
  216.5 5.8 fusion.159
  236.7 5.8 fusion.159
  256.9 5.8 fusion.159
  273.7 13.8 %all-to-all-done.1 = bf16[8,3,1,16384]{3,1,2,0:T(4,128)(2,1)S(1)} async-done(((bf16[8,3,1,16384]{3,1,2,0:T(4,128)(2,1)}), bf16[8,3,1,16384]{3,1,2,0:T(4,128)(2,1)S(1)}, u32[]{:S(2)}, u32[]{:S(2)}) %all-to-all-start.1) | async-done | bytes 786464 | tf_op jit(solution)/shard_map/all_to_all | solution.py:193
  298.1 7.1 fusion.111
  305.2 10.1 %fusion.58 = bf16[512,3072]{1,0:T(8,128)(2,1)S(1)} fusion(f32[512,3072]{1,0:T(8,128)} %fusion.111, bf16[3072,768]{0,1:T(8,128)(2,1)} %all-gather.11.cloned.1.call-done, bf16[512,768]{1,0:T(8,128)(2,1)S(1)} %copy-done.9, f32[]{:T(128)} %bitcast), kind=kOutput, calls=%fused_computation.65 | convolution fusion | flops 2448556032 | bytes 14942212 | tf_op jit(solution)/shard_map/nd,fd->nf/dot_general | solution.py:230
  318.9 15.2 %fusion.84 = (bf16[512,768]{1,0:T(8,128)(2,1)}, f32[512,768]{1,0:T(8,128)S(1)}) fusion(f32[]{:T(128)} %bitcast.39, f32[]{:T(128)} %bitcast.37, f32[]{:T(128)} %bitcast.35, f32[]{:T(128)} %bitcast.33, f32[]{:T(128)} %bitcast.31, f32[]{:T(128)} %bitcast.29, f32[]{:T(128)} %bitcast.27, f32[]{:T(128)} %bitcast.25, f32[]{:T(128)} %bitcast, ...), kind=kOutput, calls=%fused_computation.120 | convolution fusion | flops 2440691712 | bytes 21233700 | tf_op jit(solution)/shard_map/dot_general | solution.py:203
  341.1 6.5 convolution_convert_fusion.2
  347.5 6.7 copy.156
  374.5 8.8 %convolution_convert_fusion.1 = bf16[3072,768]{0,1:T(8,128)(2,1)} fusion(bf16[512,768]{1,0:T(8,128)(2,1)} %param.24, f32[]{:T(128)} %bitcast, f32[512,3072]{1,0:T(8,128)} %fusion.111), kind=kOutput, calls=%fused_computation.68 | convolution fusion | flops 2433613824 | bytes 11796484 | tf_op jit(solution)/shard_map/nf,nd->fd/dot_general | solution.py:229
  383.4 6.4 all-to-all-done.2
  396.4 239.9 %while.29 = (s32[]{:T(128)}, f32[3,2048,64]{1,2,0:T(8,128)}, f32[3,2048,64]{1,2,0:T(8,128)S(1)}, bf16[4,3,512,64]{2,3,1,0:T(8,128)(2,1)}, s32[4]{0:T(128)S(1)}, ...) while((s32[]{:T(128)}, f32[3,2048,64]{1,2,0:T(8,128)}, ...), condition=%wide.region_13.16_spmd.clone, body=%wide.region_11.15_spmd.clone.sunk | while | flops 2066226688 | bytes 200737024 | solution.py:275
  400.6 6.1 subtract_exponential_fusion.3
  411.3 6.4 fusion.170
  417.7 18.6 %fusion.173 = bf16[4,3,512,64]{2,3,1,0:T(8,128)(2,1)} fusion(bf16[4,3,512,64]{2,3,1,0:T(8,128)(2,1)} %get-tuple-element.576, s32[]{:T(128)S(6)} %copy.183, bf16[3,2048,64]{1,2,0:T(8,128)(2,1)} %get-tuple-element.594, f32[3,512,2048]{2,1,0:T(8,128)} %copy-done, f32[3,512,2048]{2,1,0:T(8,128)} %fusion.170), kind=kOutput, calls=%fused_computation.39.clone.1 | convolution fusion | flops 418385408 | bytes 51511300 | tf_op jit(solution)/shard_map/while/body/eval_jaxpr/pqk,pkd->pqd/dot_general | solution.py:263
  436.3 22.0 %fusion.171 = f32[3,2048,64]{1,2,0:T(8,128)} fusion(f32[3,512,2048]{2,1,0:T(8,128)} %copy-done, f32[3,512,2048]{2,1,0:T(8,128)} %fusion.170, f32[3,2048,64]{1,2,0:T(8,128)} %get-tuple-element.574, pred[]{:T(512)S(6)} %compare.3, bf16[3,2048,64]{1,2,0:T(8,128)(2,1)} %get-tuple-element.593, s32[]{:T(128)S(6)} %select_n.227), kind=kOutput, calls=%fused_computation.37.clone.1 | convolution fusion | flops 419171840 | bytes 53673988 | tf_op jit(solution)/shard_map/while/body/eval_jaxpr/pqk,pqd->pkd/dot_general | solution.py:266
  462.2 6.1 subtract_exponential_fusion.3
  472.9 6.4 fusion.170
  479.3 18.5 %fusion.173 = bf16[4,3,512,64]{2,3,1,0:T(8,128)(2,1)} fusion(bf16[4,3,512,64]{2,3,1,0:T(8,128)(2,1)} %get-tuple-element.576, s32[]{:T(128)S(6)} %copy.183, bf16[3,2048,64]{1,2,0:T(8,128)(2,1)} %get-tuple-element.594, f32[3,512,2048]{2,1,0:T(8,128)} %copy-done, f32[3,512,2048]{2,1,0:T(8,128)} %fusion.170), kind=kOutput, calls=%fused_computation.39.clone.1 | convolution fusion | flops 418385408 | bytes 51511300 | tf_op jit(solution)/shard_map/while/body/eval_jaxpr/pqk,pkd->pqd/dot_general | solution.py:263
  497.8 20.1 %fusion.171 = f32[3,2048,64]{1,2,0:T(8,128)} fusion(f32[3,512,2048]{2,1,0:T(8,128)} %copy-done, f32[3,512,2048]{2,1,0:T(8,128)} %fusion.170, f32[3,2048,64]{1,2,0:T(8,128)} %get-tuple-element.574, pred[]{:T(512)S(6)} %compare.3, bf16[3,2048,64]{1,2,0:T(8,128)(2,1)} %get-tuple-element.593, s32[]{:T(128)S(6)} %select_n.227), kind=kOutput, calls=%fused_computation.37.clone.1 | convolution fusion | flops 419171840 | bytes 53673988 | tf_op jit(solution)/shard_map/while/body/eval_jaxpr/pqk,pqd->pkd/dot_general | solution.py:266
  521.9 6.1 subtract_exponential_fusion.3
  532.5 6.4 fusion.170
  538.9 17.9 %fusion.173 = bf16[4,3,512,64]{2,3,1,0:T(8,128)(2,1)} fusion(bf16[4,3,512,64]{2,3,1,0:T(8,128)(2,1)} %get-tuple-element.576, s32[]{:T(128)S(6)} %copy.183, bf16[3,2048,64]{1,2,0:T(8,128)(2,1)} %get-tuple-element.594, f32[3,512,2048]{2,1,0:T(8,128)} %copy-done, f32[3,512,2048]{2,1,0:T(8,128)} %fusion.170), kind=kOutput, calls=%fused_computation.39.clone.1 | convolution fusion | flops 418385408 | bytes 51511300 | tf_op jit(solution)/shard_map/while/body/eval_jaxpr/pqk,pkd->pqd/dot_general | solution.py:263
  556.8 20.1 %fusion.171 = f32[3,2048,64]{1,2,0:T(8,128)} fusion(f32[3,512,2048]{2,1,0:T(8,128)} %copy-done, f32[3,512,2048]{2,1,0:T(8,128)} %fusion.170, f32[3,2048,64]{1,2,0:T(8,128)} %get-tuple-element.574, pred[]{:T(512)S(6)} %compare.3, bf16[3,2048,64]{1,2,0:T(8,128)(2,1)} %get-tuple-element.593, s32[]{:T(128)S(6)} %select_n.227), kind=kOutput, calls=%fused_computation.37.clone.1 | convolution fusion | flops 419171840 | bytes 53673988 | tf_op jit(solution)/shard_map/while/body/eval_jaxpr/pqk,pqd->pkd/dot_general | solution.py:266
  580.9 6.1 subtract_exponential_fusion.3
  591.6 6.4 fusion.170
  598.0 17.9 %fusion.173 = bf16[4,3,512,64]{2,3,1,0:T(8,128)(2,1)} fusion(bf16[4,3,512,64]{2,3,1,0:T(8,128)(2,1)} %get-tuple-element.576, s32[]{:T(128)S(6)} %copy.183, bf16[3,2048,64]{1,2,0:T(8,128)(2,1)} %get-tuple-element.594, f32[3,512,2048]{2,1,0:T(8,128)} %copy-done, f32[3,512,2048]{2,1,0:T(8,128)} %fusion.170), kind=kOutput, calls=%fused_computation.39.clone.1 | convolution fusion | flops 418385408 | bytes 51511300 | tf_op jit(solution)/shard_map/while/body/eval_jaxpr/pqk,pkd->pqd/dot_general | solution.py:263
  615.9 20.0 %fusion.171 = f32[3,2048,64]{1,2,0:T(8,128)} fusion(f32[3,512,2048]{2,1,0:T(8,128)} %copy-done, f32[3,512,2048]{2,1,0:T(8,128)} %fusion.170, f32[3,2048,64]{1,2,0:T(8,128)} %get-tuple-element.574, pred[]{:T(512)S(6)} %compare.3, bf16[3,2048,64]{1,2,0:T(8,128)(2,1)} %get-tuple-element.593, s32[]{:T(128)S(6)} %select_n.227), kind=kOutput, calls=%fused_computation.37.clone.1 | convolution fusion | flops 419171840 | bytes 53673988 | tf_op jit(solution)/shard_map/while/body/eval_jaxpr/pqk,pqd->pkd/dot_general | solution.py:266
  663.1 35.9 %all-to-all-done.3 = bf16[8,3,3,16384]{3,1,2,0:T(4,128)(2,1)S(1)} async-done(((bf16[8,3,3,16384]{3,1,2,0:T(4,128)(2,1)}), bf16[8,3,3,16384]{3,1,2,0:T(4,128)(2,1)S(1)}, u32[]{:S(2)}, u32[]{:S(2)}) %all-to-all-start.3) | async-done | bytes 2359328 | tf_op jit(solution)/shard_map/all_to_all | solution.py:280
  703.1 6.9 gather_fusion.4
  713.2 8.4 reshape.610
  721.6 6.5 copy.142
  748.6 5.6 stack.69
  755.9 31.1 %reduce-scatter.15.cloned.1.call-done = bf16[768,288]{0,1:T(8,128)(2,1)} async-done(((bf16[768,2304]{0,1:T(8,128)(2,1)}), bf16[768,288]{0,1:T(8,128)(2,1)}) %reduce-scatter.15.cloned.1.call-update) | async-done | bytes 442384 | tf_op jit(solution)/shard_map/reduce_scatter | solution.py:293
  789.1 6.3 fusion.74
  795.4 40.4 %all-reduce = (f32[768]{0:T(1024)}, f32[768]{0:T(1024)}, f32[768]{0:T(1024)}, f32[768]{0:T(1024)}, f32[9]{0:T(128)}) all-reduce(f32[768]{0:T(1024)S(1)} %get-tuple-element.307, f32[768]{0:T(1024)S(1)} %get-tuple-element.312, f32[768]{0:T(1024)S(1)} %copy-done.29, ...), channel_id=1, replica_groups=mesh['batch'=4,'seq'=8] {'batch','seq'}, use_global_device_ids=true, to_apply=%region_25.28 | all-reduce | flops 3081 | bytes 24648 | tf_op jit(solution)/shard_map/psum | solution.py:320
  842.0 15.0 %reduce-scatter.25.cloned.1.call-done = bf16[192,288]{1,0:T(8,128)(2,1)} async-done(((bf16[768,288]{1,0:T(8,128)(2,1)}), bf16[192,288]{1,0:T(8,128)(2,1)}) %reduce-scatter.25.cloned.1.call-update) | async-done | bytes 110608
  (315 shorter events, 252.1 us)
Async XLA Ops:
  7.2 34.5 %copy-start.18 = (bf16[192,384]{1,0:T(8,128)(2,1)S(1)}, bf16[192,384]{1,0:T(8,128)(2,1)}, u32[]{:S(2)}) copy-start(bf16[192,384]{1,0:T(8,128)(2,1)} %param.27) | copy-start | bytes 442372
  7.2 51.6 %copy-start.44 = (s32[1,2]{1,0:T(1,128)S(1)}, s32[1,2]{1,0:T(1,128)}, u32[]{:S(2)}) copy-start(s32[1,2]{1,0:T(1,128)} %param.35) | copy-start | bytes 28
  7.2 51.7 %copy-start.37 = (s32[1,24]{1,0:T(1,128)S(1)}, s32[1,24]{1,0:T(1,128)}, u32[]{:S(2)}) copy-start(s32[1,24]{1,0:T(1,128)} %param.34) | copy-start | bytes 292
  7.2 51.8 %copy-start.3 = (bf16[512,768]{1,0:T(8,128)(2,1)S(1)}, bf16[512,768]{1,0:T(8,128)(2,1)}, u32[]{:S(2)}) copy-start(bf16[512,768]{1,0:T(8,128)(2,1)} %param.22) | copy-start | bytes 2359300
  7.2 55.3 %all-gather.5.cloned.1.call-start = ((), (), s32[]{:S(2)}) async-start(), calls=%async_computation.12 | async-start | bytes 3981312 | tf_op jit(solution)/shard_map/all_gather | solution.py:143
  26.9 35.7 %copy-start.31 = (f32[768]{0:T(1024)S(1)}, f32[768]{0:T(1024)}, u32[]{:S(2)}) copy-start(f32[768]{0:T(1024)} %param.29) | copy-start | bytes 9220
  26.9 35.7 %copy-start.42 = (f32[768]{0:T(1024)S(1)}, f32[768]{0:T(1024)}, u32[]{:S(2)}) copy-start(f32[768]{0:T(1024)} %param.30) | copy-start | bytes 9220
  26.9 268.4 %all-gather.7.cloned.1.call-start = ((), (), s32[]{:S(2)}) async-start(), calls=%async_computation.13 | async-start | bytes 1327104 | tf_op jit(solution)/shard_map/all_gather | solution.py:144
  41.6 256.5 %all-gather.9.cloned.1.call-start = ((), (), s32[]{:S(2)}) async-start(), calls=%async_computation.14 | async-start | bytes 5308416 | tf_op jit(solution)/shard_map/all_gather | solution.py:145
  59.2 7.5 copy-start.22
  62.5 14.6 %copy-start.13 = (f32[2,256,32]{1,0,2:T(2,128)}, f32[2,256,32]{1,0,2:T(2,128)S(1)}, u32[]{:S(2)}) copy-start(f32[2,256,32]{1,0,2:T(2,128)S(1)} %get-tuple-element.381) | copy-start | bytes 196612
  62.5 14.6 %copy-start.15 = (f32[2,256,32]{1,0,2:T(2,128)}, f32[2,256,32]{1,0,2:T(2,128)S(1)}, u32[]{:S(2)}) copy-start(f32[2,256,32]{1,0,2:T(2,128)S(1)} %get-tuple-element.382) | copy-start | bytes 196612
  62.5 36.9 %copy-start.26 = (s32[1024]{0:T(1024)}, s32[1024]{0:T(1024)S(1)}, u32[]{:S(2)}) copy-start(s32[1024]{0:T(1024)S(1)} %get-tuple-element.404) | copy-start | bytes 12292
  62.5 44.1 %copy-start.33 = (pred[24]{0:T(512)(128)(4,1)}, pred[24]{0:T(512)(128)(4,1)S(1)}, u32[]{:S(2)}) copy-start(pred[24]{0:T(512)(128)(4,1)S(1)} %compare_and_fusion.1) | copy-start | bytes 76
  62.5 4.2 copy-start.24
  112.2 3.9 copy-start.19
  112.2 49.9 %all-to-all-start = ((bf16[8,3,3,16384]{3,1,2,0:T(4,128)(2,1)}), bf16[8,3,3,16384]{3,1,2,0:T(4,128)(2,1)S(1)}, u32[]{:S(2)}, u32[]{:S(2)}) async-start(bf16[8,3,3,16384]{3,1,2,0:T(4,128)(2,1)} %copy.121), calls=%async_computation | async-start | bytes 6291456 | tf_op jit(solution)/shard_map/all_to_all | solution.py:158
  116.0 189.2 %all-gather.11.cloned.1.call-start = ((), (), s32[]{:S(2)}) async-start(), calls=%async_computation.15 | async-start | bytes 5308416 | tf_op jit(solution)/shard_map/all_gather | solution.py:146
  267.0 5.3 copy-start.38
  267.0 6.0 copy-start.20
  268.7 18.9 %all-to-all-start.1 = ((bf16[8,3,1,16384]{3,1,2,0:T(4,128)(2,1)}), bf16[8,3,1,16384]{3,1,2,0:T(4,128)(2,1)S(1)}, u32[]{:S(2)}, u32[]{:S(2)}) async-start(bf16[8,3,1,16384]{3,1,2,0:T(4,128)(2,1)} %copy.127), calls=%async_computation.1 | async-start | bytes 2097152 | tf_op jit(solution)/shard_map/all_to_all | solution.py:193
  272.2 389.1 %reduce-scatter.17.cloned.1.call-start = ((), (), s32[]{:S(2)}) async-start(), calls=%async_computation.17 | async-start | bytes 1327104 | tf_op jit(solution)/shard_map/reduce_scatter | solution.py:296
  273.0 16.3 %copy-start.27 = (s32[1024]{0:T(1024)}, s32[1024]{0:T(1024)S(1)}, u32[]{:S(2)}) copy-start(s32[1024]{0:T(1024)S(1)} %pad_clamp_fusion) | copy-start | bytes 12292
  273.7 15.6 %copy-start.35 = (pred[24]{0:T(512)(128)(4,1)}, pred[24]{0:T(512)(128)(4,1)S(1)}, u32[]{:S(2)}) copy-start(pred[24]{0:T(512)(128)(4,1)S(1)} %compare_and_fusion) | copy-start | bytes 76
  291.1 4.2 copy-start.4
  298.0 7.2 copy-start.9
  305.2 10.1 %copy-start.39 = (bf16[768,3072]{1,0:T(8,128)(2,1)S(1)}, bf16[768,3072]{1,0:T(8,128)(2,1)}, u32[]{:S(2)}) copy-start(bf16[768,3072]{1,0:T(8,128)(2,1)} %all-gather.9.cloned.1.call-done) | copy-start | bytes 14155780
  318.9 15.2 %slice-start = ((s8[6291456]{0:T(1024)(128)(4,1)}), s8[4194304]{0:T(1024)(128)(4,1)S(1)}, s32[]{:S(2)}) async-start(s8[6291456]{0:T(1024)(128)(4,1)} %bitcast.246), calls=%async_computation.24 | async-start | bytes 8388608
  318.9 15.2 %slice-start.1 = ((s8[6291456]{0:T(1024)(128)(4,1)}), s8[2097152]{0:T(1024)(128)(4,1)S(1)}, s32[]{:S(2)}) async-start(s8[6291456]{0:T(1024)(128)(4,1)} %bitcast.246), calls=%async_computation.25 | async-start | bytes 4194304
  318.9 15.2 %copy-start.10 = (bf16[512,768]{1,0:T(8,128)(2,1)S(1)}, bf16[512,768]{1,0:T(8,128)(2,1)}, u32[]{:S(2)}) copy-start(bf16[512,768]{1,0:T(8,128)(2,1)} %param.24) | copy-start | bytes 2359300
  334.1 4.9 copy-start.6
  341.0 398.9 %reduce-scatter.29.cloned.1.call-start = ((), (), s32[]{:S(2)}) async-start(), calls=%async_computation.23 | async-start | bytes 5308416
  370.9 18.9 %all-to-all-start.2 = ((bf16[8,3,1,16384]{3,1,2,0:T(4,128)(2,1)}), bf16[8,3,1,16384]{3,1,2,0:T(4,128)(2,1)S(1)}, u32[]{:S(2)}, u32[]{:S(2)}) async-start(bf16[8,3,1,16384]{3,1,2,0:T(4,128)(2,1)} %bitcast.250), calls=%async_computation.2 | async-start | bytes 2097152 | tf_op jit(solution)/shard_map/all_to_all | solution.py:242
  374.5 367.8 %reduce-scatter.21.cloned.1.call-start = ((), (), s32[]{:S(2)}) async-start(), calls=%async_computation.19 | async-start | bytes 5308416 | tf_op jit(solution)/shard_map/reduce_scatter | solution.py:302
  406.8 4.5 copy-start
  468.4 4.5 copy-start
  528.0 4.5 copy-start
  587.0 4.5 copy-start
  657.6 41.4 %all-to-all-start.3 = ((bf16[8,3,3,16384]{3,1,2,0:T(4,128)(2,1)}), bf16[8,3,3,16384]{3,1,2,0:T(4,128)(2,1)S(1)}, u32[]{:S(2)}, u32[]{:S(2)}) async-start(bf16[8,3,3,16384]{3,1,2,0:T(4,128)(2,1)} %copy.138), calls=%async_computation.3 | async-start | bytes 6291456 | tf_op jit(solution)/shard_map/all_to_all | solution.py:280
  661.2 93.0 %reduce-scatter.27.cloned.1.call-start = ((), (), s32[]{:S(2)}) async-start(), calls=%async_computation.22 | async-start | bytes 245760
  663.1 123.9 %reduce-scatter.15.cloned.1.call-start = ((), (), s32[]{:S(2)}) async-start(), calls=%async_computation.16 | async-start | bytes 3981312 | tf_op jit(solution)/shard_map/reduce_scatter | solution.py:293
  703.1 7.0 copy-start.36
  739.9 98.8 %reduce-scatter.19.cloned.1.call-start = ((), (), s32[]{:S(2)}) async-start(), calls=%async_computation.18 | async-start | bytes 737280 | tf_op jit(solution)/shard_map/reduce_scatter | solution.py:313
  742.2 98.2 %reduce-scatter.23.cloned.1.call-start = ((), (), s32[]{:S(2)}) async-start(), calls=%async_computation.20 | async-start | bytes 737280 | tf_op jit(solution)/shard_map/reduce_scatter | solution.py:316
  742.9 114.1 %reduce-scatter.25.cloned.1.call-start = ((), (), s32[]{:S(2)}) async-start(), calls=%async_computation.21 | async-start | bytes 737280
  789.1 6.4 copy-start.29
  789.1 6.4 copy-start.30
  789.1 46.8 %copy-start.2 = (f32[512,768]{1,0:T(8,128)S(1)}, f32[512,768]{1,0:T(8,128)}, u32[]{:S(2)}) copy-start(f32[512,768]{1,0:T(8,128)} %copy-done.1) | copy-start | bytes 4718596
  (19 other events, 43.1 us)
Sparse Core Ops, SparseCore 0:
  27.0 35.0 all-gather.4
  64.5 23.9 all-gather.6
  90.4 47.8 all-gather.8
  139.9 55.3 all-gather.10
  341.1 35.5 reduce-scatter.16
  380.0 53.7 reduce-scatter.28
  437.3 53.7 reduce-scatter.20
  664.9 20.7 reduce-scatter.26
  740.0 46.9 reduce-scatter.14
  789.1 22.1 reduce-scatter.18
  813.6 20.6 reduce-scatter.22
  836.4 20.6 reduce-scatter.24
where the time goes:
time: 872 us; the launch traced here: 866 us
  matrix products  330 us (38%)
  local copies, waits for them, and re-layouts  179 us (21%)
  waiting for transfers between devices  131 us (15%)
  blocking collectives  107 us (12%)
  other arithmetic  71.9 us (8%)
  loops' own time  16.5 us (2%)
  between operations  15.6 us (2%)
  starting transfers between devices  15.3 us (2%)
    dot_general x4, matrix products, backward_block(): jnp.einsum('pqk,pqd->pkd', dscore, query_block, preferred_element_type=jn...  82.2 us
    dot_general x4, matrix products, backward_block(): jnp.einsum('pqk,pkd->pqd', dscore, key_pairs, preferred_element_type=jnp....  72.8 us
    dot_general x8, matrix products, masked_scores(): jnp.einsum('pqd,pkd->pqk', query_block, key_pairs, preferred_element_type...  46.4 us
    psum x1, blocking collectives, local(): lax.psum((gain1_local, bias1_local, gain2_local, bias2_local, dwa_local),...  40.4 us
    all_to_all x1, waiting for transfers between devices, local(): lax.all_to_all(pairs_split(dpairs, n_seq), 'seq', split_axis=0, concat_ax...  35.9 us
    reduce_scatter x1, waiting for transfers between devices, local(): lax.psum_scatter(qkv_local.astype(jnp.bfloat16), 'seq', scatter_dimension...  31.1 us
    unnamed x112, local copies, waits for them, and re-layouts  29.7 us
    all_to_all x1, waiting for transfers between devices, local(): lax.all_to_all(to_pairs(stacked, order_row, n_seq, per_dev), 'seq', split...  27.8 us
  transfers between devices with their start and end apart: 16, of which 6 were waited for; matrix products, arithmetic and copies ran while one was open for 61% of the time, Pallas kernels for 0%

commit v1 on v0

--- a/solution.py
+++ b/solution.py
@@ -10,6 +10,19 @@
 HIST = 8
 NORM_EPS = 1e-05
 MASKED = -1e30
+
+
+def cube_check(state, ndim_at, m):
+    small, arr_out = (state.shape[:ndim_at], state.shape[ndim_at + 1 :])
+    low = jnp.moveaxis(state.reshape(*small, m, -1, *arr_out), ndim_at, 0)
+    return low
+
+
+def samples_all_define(local_block, dim_at):
+    reached = list(local_block.shape[1:])
+    reached[dim_at] *= local_block.shape[0]
+    local_next = jnp.moveaxis(local_block, 0, dim_at).reshape(reached)
+    return local_next
 
 
 def norm_rows(values, gain, shift):
@@ -105,6 +118,21 @@
     pair_order,
     long_group,
 ):
+
+    def bring_local_data(x_in, link_axis, a0, block_here):
+        state_next = lax.axis_size(link_axis)
+        all_values = lax.axis_index(link_axis)
+        g_now, carry_in = (state_next, all_values)
+        u_next = cube_check(x_in, a0, g_now)
+        in_order = [u_next[carry_in]]
+        for w in range(1, g_now):
+            right_arr = u_next[carry_in ^ w]
+            f_next = lax.ppermute(right_arr, link_axis, [(i, i ^ w) for i in range(g_now)])
+            in_order.append(f_next)
+        u_next = jnp.stack(in_order)[carry_in ^ jnp.arange(g_now)]
+        raw_out = samples_all_define(u_next, block_here)
+        return raw_out
+
     n_seq = lax.axis_size("seq")
     row_count = block_input.shape[0]
     piece_len = SLOT // n_seq
@@ -277,9 +305,7 @@
     )
     dquery = jnp.transpose(dquery_blocks, (1, 0, 2, 3)).reshape(per_dev, SLOT, HD)
     dpairs = jnp.stack([dquery, dkeys_sum, dvalues_sum], axis=1).astype(jnp.bfloat16)
-    dreturned = lax.all_to_all(
-        pairs_split(dpairs, n_seq), "seq", split_axis=0, concat_axis=0, tiled=True
-    )
+    dreturned = bring_local_data(pairs_split(dpairs, n_seq), "seq", 0, block_here=0)
     dtokens = tokens_back(dreturned, inverse, slot_count, HD)
     dq_rows = unrotate(dtokens[:, :, 0].astype(jnp.float32), cosine, sine_tab).reshape(row_count, D)
     dk_rows = unrotate(dtokens[:, :, 1].astype(jnp.float32), cosine, sine_tab).reshape(row_count, D)

time: 872 us -> 982 us (1.13)
  waiting for transfers between devices: 131 us -> 241 us
    reduce_scatter x1, waiting for transfers between devices: 0.02 us -> 44.2 us  [local(): lax.psum_scatter(down_local.astype(jnp.bfloat16), 'seq', scatter_dimensio...]
    unnamed x15, waiting for transfers between devices: 15.9 us -> 55.3 us
    all_to_all x1 -> x0, waiting for transfers between devices: 35.9 us -> none  [local(): lax.all_to_all(pairs_split(dpairs, n_seq), 'seq', split_axis=0, concat_ax...]
    ppermute x0 -> x7, waiting for transfers between devices: none -> 31.7 us  [bring_local_data(): lax.ppermute(right_arr, link_axis, [(i, i ^ w) for i in range(g_now)])]
    reduce_scatter x1, waiting for transfers between devices: 0.01 us -> 21.2 us  [local(): lax.psum_scatter(col_sums[3].astype(jnp.bfloat16), 'batch', scatter_dimen...]
    reduce_scatter x1, waiting for transfers between devices: 0.01 us -> 15 us  [local(): lax.psum_scatter(col_sums[2].astype(jnp.bfloat16), 'batch', scatter_dimen...]
    reduce_scatter x1, waiting for transfers between devices: 31.1 us -> 20.8 us  [local(): lax.psum_scatter(qkv_local.astype(jnp.bfloat16), 'seq', scatter_dimension...]
    unnamed x112 -> x139, local copies, waits for them, and re-layouts: 29.7 us -> 35.9 us
  transfers between devices with their start and end apart: 16 -> 22, of which waited for: 6 -> 11; matrix products, arithmetic and copies ran while one was open for 61% -> 53% of each run, Pallas kernels for 0% -> 0%
where the time goes in v1:
time: 982 us; the launch traced here: 977 us
  matrix products  325 us (33%)
  waiting for transfers between devices  241 us (25%)
  local copies, waits for them, and re-layouts  184 us (19%)
  blocking collectives  107 us (11%)
  other arithmetic  70.7 us (7%)
  loops' own time  16.7 us (2%)
  starting transfers between devices  16 us (2%)
  between operations  15.9 us (2%)
    dot_general x4, matrix products, backward_block(): jnp.einsum('pqk,pqd->pkd', dscore, query_block, preferred_element_type=jn...  79.8 us
    dot_general x4, matrix products, backward_block(): jnp.einsum('pqk,pkd->pqd', dscore, key_pairs, preferred_element_type=jnp....  71.7 us
    unnamed x15, waiting for transfers between devices  55.3 us
    dot_general x8, matrix products, masked_scores(): jnp.einsum('pqd,pkd->pqk', query_block, key_pairs, preferred_element_type...  46.4 us
    reduce_scatter x1, waiting for transfers between devices, local(): lax.psum_scatter(down_local.astype(jnp.bfloat16), 'seq', scatter_dimensio...  44.2 us
    psum x1, blocking collectives, local(): lax.psum((gain1_local, bias1_local, gain2_local, bias2_local, dwa_local),...  40.4 us
    unnamed x139, local copies, waits for them, and re-layouts  35.9 us
    ppermute x7, waiting for transfers between devices, bring_local_data(): lax.ppermute(right_arr, link_axis, [(i, i ^ w) for i in range(g_now)])  31.7 us
  transfers between devices with their start and end apart: 22, of which 11 were waited for; matrix products, arithmetic and copies ran while one was open for 53% of the time, Pallas kernels for 0%

profile of v1, /device:TPU:0, one launch (start us, length us, event | category | flops | bytes accessed | tf_op | source)
XLA Modules:
  0.0 976.5 jit_solution(8724100538782581522)
XLA Ops:
  7.3 18.6 %all_gather.32 = bf16[768,288]{1,0:T(8,128)(2,1)S(1)} all-gather(bf16[192,288]{1,0:T(8,128)(2,1)} %param.25), channel_id=1, replica_groups=mesh['batch'=4,'seq'=8] {'batch'}, dimensions={0}, use_global_device_ids=true | all-gather | bytes 552960 | tf_op jit(solution)/shard_map/all_gather | solution.py:165
  27.0 13.8 %all_gather.34 = bf16[768,96]{1,0:T(8,128)(2,1)S(1)} all-gather(bf16[192,96]{1,0:T(8,128)(2,1)} %param.26), channel_id=1, replica_groups=mesh['batch'=4,'seq'=8] {'batch'}, dimensions={0}, use_global_device_ids=true | all-gather | bytes 184320 | tf_op jit(solution)/shard_map/all_gather | solution.py:166
  41.7 17.0 %all_gather.36 = bf16[768,384]{1,0:T(8,128)(2,1)} all-gather(bf16[192,384]{1,0:T(8,128)(2,1)S(1)} %copy-done.20), channel_id=1, replica_groups=mesh['batch'=4,'seq'=8] {'batch'}, dimensions={0}, use_global_device_ids=true | all-gather | bytes 737280 | tf_op jit(solution)/shard_map/all_gather | solution.py:167
  91.2 8.1 reshape.655
  99.4 7.2 gather_fusion.2
  116.1 17.4 %all_gather.38 = bf16[3072,96]{0,1:T(8,128)(2,1)} all-gather(bf16[768,96]{0,1:T(8,128)(2,1)S(1)} %copy-done.21), channel_id=1, replica_groups=mesh['batch'=4,'seq'=8] {'batch'}, dimensions={0}, use_global_device_ids=true | all-gather | bytes 737280 | tf_op jit(solution)/shard_map/all_gather | solution.py:168
  134.2 27.8 %all-to-all-done = bf16[8,3,3,16384]{3,1,2,0:T(4,128)(2,1)S(1)} async-done(((bf16[8,3,3,16384]{3,1,2,0:T(4,128)(2,1)}), bf16[8,3,3,16384]{3,1,2,0:T(4,128)(2,1)S(1)}, u32[]{:S(2)}, u32[]{:S(2)}) %all-to-all-start) | async-done | bytes 2359328 | tf_op jit(solution)/shard_map/all_to_all | solution.py:186
  165.2 7.1 reshape.553
  181.9 80.9 %while.28 = (s32[]{:T(128)}, bf16[4,3,512,64]{2,3,1,0:T(8,128)(2,1)}, f32[4,3,512]{2,1,0:T(4,128)S(1)}, s32[4]{0:T(128)S(1)}, s32[3,2048]{1,0:T(4,128)S(1)}, /*i...) while((s32[]{:T(128)}, ...), condition=%wide.region_5.7_spmd.clone, body=%wide.region_2.6_spmd.clone.sunk | while | flops 863075328 | bytes 44073140 | solution.py:218
  256.9 5.8 fusion.160
  273.4 13.9 %all-to-all-done.1 = bf16[8,3,1,16384]{3,1,2,0:T(4,128)(2,1)S(1)} async-done(((bf16[8,3,1,16384]{3,1,2,0:T(4,128)(2,1)}), bf16[8,3,1,16384]{3,1,2,0:T(4,128)(2,1)S(1)}, u32[]{:S(2)}, u32[]{:S(2)}) %all-to-all-start.1) | async-done | bytes 786464 | tf_op jit(solution)/shard_map/all_to_all | solution.py:221
  297.9 7.3 fusion.112
  305.2 10.1 %fusion.58 = bf16[512,3072]{1,0:T(8,128)(2,1)S(1)} fusion(f32[512,3072]{1,0:T(8,128)} %fusion.112, bf16[3072,768]{0,1:T(8,128)(2,1)} %all-gather.11.cloned.1.call-done, bf16[512,768]{1,0:T(8,128)(2,1)S(1)} %copy-done.12, f32[]{:T(128)} %bitcast), kind=kOutput, calls=%fused_computation.66 | convolution fusion | flops 2448556032 | bytes 14942212 | tf_op jit(solution)/shard_map/nd,fd->nf/dot_general | solution.py:258
  318.8 14.8 %fusion.84 = (bf16[512,768]{1,0:T(8,128)(2,1)}, f32[512,768]{1,0:T(8,128)S(1)}) fusion(f32[]{:T(128)} %bitcast.39, f32[]{:T(128)} %bitcast.37, f32[]{:T(128)} %bitcast.35, f32[]{:T(128)} %bitcast.33, f32[]{:T(128)} %bitcast.31, f32[]{:T(128)} %bitcast.29, f32[]{:T(128)} %bitcast.27, f32[]{:T(128)} %bitcast.25, f32[]{:T(128)} %bitcast, ...), kind=kOutput, calls=%fused_computation.120 | convolution fusion | flops 2440691712 | bytes 21233700 | tf_op jit(solution)/shard_map/dot_general | solution.py:231
  355.5 10.9 %all-to-all-done.2 = bf16[8,3,1,16384]{3,1,2,0:T(4,128)(2,1)S(1)} async-done(((bf16[8,3,1,16384]{3,1,2,0:T(4,128)(2,1)}), bf16[8,3,1,16384]{3,1,2,0:T(4,128)(2,1)S(1)}, u32[]{:S(2)}, u32[]{:S(2)}) %all-to-all-start.2) | async-done | bytes 786464 | tf_op jit(solution)/shard_map/all_to_all | solution.py:270
  373.0 237.2 %while.29 = (s32[]{:T(128)}, f32[3,2048,64]{1,2,0:T(8,128)}, f32[3,2048,64]{1,2,0:T(8,128)S(1)}, bf16[4,3,512,64]{2,3,1,0:T(8,128)(2,1)}, s32[4]{0:T(128)S(1)}, ...) while((s32[]{:T(128)}, f32[3,2048,64]{1,2,0:T(8,128)}, ...), condition=%wide.region_13.16_spmd.clone, body=%wide.region_11.15_spmd.clone.sunk | while | flops 2066226688 | bytes 200737024 | solution.py:303
  377.4 6.1 subtract_exponential_fusion.3
  388.1 6.4 fusion.171
  394.5 17.9 %fusion.174 = bf16[4,3,512,64]{2,3,1,0:T(8,128)(2,1)} fusion(bf16[4,3,512,64]{2,3,1,0:T(8,128)(2,1)} %get-tuple-element.584, s32[]{:T(128)S(6)} %copy.219, bf16[3,2048,64]{1,2,0:T(8,128)(2,1)} %get-tuple-element.602, f32[3,512,2048]{2,1,0:T(8,128)} %copy-done, f32[3,512,2048]{2,1,0:T(8,128)} %fusion.171), kind=kOutput, calls=%fused_computation.40.clone.1 | convolution fusion | flops 418385408 | bytes 51511300 | tf_op jit(solution)/shard_map/while/body/eval_jaxpr/pqk,pkd->pqd/dot_general | solution.py:291
  412.4 19.6 %fusion.172 = f32[3,2048,64]{1,2,0:T(8,128)} fusion(f32[3,512,2048]{2,1,0:T(8,128)} %copy-done, f32[3,512,2048]{2,1,0:T(8,128)} %fusion.171, f32[3,2048,64]{1,2,0:T(8,128)} %get-tuple-element.582, pred[]{:T(512)S(6)} %compare.3, bf16[3,2048,64]{1,2,0:T(8,128)(2,1)} %get-tuple-element.601, s32[]{:T(128)S(6)} %select_n.273), kind=kOutput, calls=%fused_computation.38.clone.1 | convolution fusion | flops 419171840 | bytes 53673988 | tf_op jit(solution)/shard_map/while/body/eval_jaxpr/pqk,pqd->pkd/dot_general | solution.py:294
  436.3 6.1 subtract_exponential_fusion.3
  446.9 6.4 fusion.171
  453.4 17.9 %fusion.174 = bf16[4,3,512,64]{2,3,1,0:T(8,128)(2,1)} fusion(bf16[4,3,512,64]{2,3,1,0:T(8,128)(2,1)} %get-tuple-element.584, s32[]{:T(128)S(6)} %copy.219, bf16[3,2048,64]{1,2,0:T(8,128)(2,1)} %get-tuple-element.602, f32[3,512,2048]{2,1,0:T(8,128)} %copy-done, f32[3,512,2048]{2,1,0:T(8,128)} %fusion.171), kind=kOutput, calls=%fused_computation.40.clone.1 | convolution fusion | flops 418385408 | bytes 51511300 | tf_op jit(solution)/shard_map/while/body/eval_jaxpr/pqk,pkd->pqd/dot_general | solution.py:291
  471.3 20.1 %fusion.172 = f32[3,2048,64]{1,2,0:T(8,128)} fusion(f32[3,512,2048]{2,1,0:T(8,128)} %copy-done, f32[3,512,2048]{2,1,0:T(8,128)} %fusion.171, f32[3,2048,64]{1,2,0:T(8,128)} %get-tuple-element.582, pred[]{:T(512)S(6)} %compare.3, bf16[3,2048,64]{1,2,0:T(8,128)(2,1)} %get-tuple-element.601, s32[]{:T(128)S(6)} %select_n.273), kind=kOutput, calls=%fused_computation.38.clone.1 | convolution fusion | flops 419171840 | bytes 53673988 | tf_op jit(solution)/shard_map/while/body/eval_jaxpr/pqk,pqd->pkd/dot_general | solution.py:294
  495.6 6.1 subtract_exponential_fusion.3
  506.3 6.4 fusion.171
  512.7 17.9 %fusion.174 = bf16[4,3,512,64]{2,3,1,0:T(8,128)(2,1)} fusion(bf16[4,3,512,64]{2,3,1,0:T(8,128)(2,1)} %get-tuple-element.584, s32[]{:T(128)S(6)} %copy.219, bf16[3,2048,64]{1,2,0:T(8,128)(2,1)} %get-tuple-element.602, f32[3,512,2048]{2,1,0:T(8,128)} %copy-done, f32[3,512,2048]{2,1,0:T(8,128)} %fusion.171), kind=kOutput, calls=%fused_computation.40.clone.1 | convolution fusion | flops 418385408 | bytes 51511300 | tf_op jit(solution)/shard_map/while/body/eval_jaxpr/pqk,pkd->pqd/dot_general | solution.py:291
  530.6 20.1 %fusion.172 = f32[3,2048,64]{1,2,0:T(8,128)} fusion(f32[3,512,2048]{2,1,0:T(8,128)} %copy-done, f32[3,512,2048]{2,1,0:T(8,128)} %fusion.171, f32[3,2048,64]{1,2,0:T(8,128)} %get-tuple-element.582, pred[]{:T(512)S(6)} %compare.3, bf16[3,2048,64]{1,2,0:T(8,128)(2,1)} %get-tuple-element.601, s32[]{:T(128)S(6)} %select_n.273), kind=kOutput, calls=%fused_computation.38.clone.1 | convolution fusion | flops 419171840 | bytes 53673988 | tf_op jit(solution)/shard_map/while/body/eval_jaxpr/pqk,pqd->pkd/dot_general | solution.py:294
  555.0 6.1 subtract_exponential_fusion.3
  565.6 6.4 fusion.171
  572.0 17.9 %fusion.174 = bf16[4,3,512,64]{2,3,1,0:T(8,128)(2,1)} fusion(bf16[4,3,512,64]{2,3,1,0:T(8,128)(2,1)} %get-tuple-element.584, s32[]{:T(128)S(6)} %copy.219, bf16[3,2048,64]{1,2,0:T(8,128)(2,1)} %get-tuple-element.602, f32[3,512,2048]{2,1,0:T(8,128)} %copy-done, f32[3,512,2048]{2,1,0:T(8,128)} %fusion.171), kind=kOutput, calls=%fused_computation.40.clone.1 | convolution fusion | flops 418385408 | bytes 51511300 | tf_op jit(solution)/shard_map/while/body/eval_jaxpr/pqk,pkd->pqd/dot_general | solution.py:291
  590.0 20.1 %fusion.172 = f32[3,2048,64]{1,2,0:T(8,128)} fusion(f32[3,512,2048]{2,1,0:T(8,128)} %copy-done, f32[3,512,2048]{2,1,0:T(8,128)} %fusion.171, f32[3,2048,64]{1,2,0:T(8,128)} %get-tuple-element.582, pred[]{:T(512)S(6)} %compare.3, bf16[3,2048,64]{1,2,0:T(8,128)(2,1)} %get-tuple-element.601, s32[]{:T(128)S(6)} %select_n.273), kind=kOutput, calls=%fused_computation.38.clone.1 | convolution fusion | flops 419171840 | bytes 53673988 | tf_op jit(solution)/shard_map/while/body/eval_jaxpr/pqk,pqd->pkd/dot_general | solution.py:294
  627.6 6.4 constant_dynamic-slice_fusion.3
  641.9 6.4 collective-permute-done.1
  648.4 7.2 collective-permute-done.2
  656.0 18.1 %collective-permute-done.4 = bf16[1,3,3,16384]{3,2,1,0:T(4,128)(2,1)S(1)} collective-permute-done((bf16[1,3,3,16384]{3,2,1,0:T(4,128)(2,1)S(1)}, bf16[1,3,3,16384]{3,2,1,0:T(4,128)(2,1)S(1)}, u32[]{:S(2)}, u32[]{:S(2)}) %collective-permute-start.4) | collective-permute-done | bytes 294944 | tf_op jit(solution)/shard_map/ppermute | solution.py:130
  690.5 6.3 reshape.658
  696.8 6.5 copy.165
  716.6 6.5 convolution_convert_fusion.2
  723.1 6.8 copy.178
  731.0 8.6 convolution_convert_fusion.1
  741.6 20.8 %reduce-scatter.15.cloned.1.call-done = bf16[768,288]{0,1:T(8,128)(2,1)} async-done(((bf16[768,2304]{0,1:T(8,128)(2,1)}), bf16[768,288]{0,1:T(8,128)(2,1)}) %reduce-scatter.15.cloned.1.call-update) | async-done | bytes 442384 | tf_op jit(solution)/shard_map/reduce_scatter | solution.py:319
  764.5 55.1 %reduce-scatter.29.cloned.1.call-done = bf16[384,768]{1,0:T(8,128)(2,1)} async-done(((bf16[3072,768]{1,0:T(8,128)(2,1)}), bf16[384,768]{1,0:T(8,128)(2,1)}) %reduce-scatter.29.cloned.1.call-update) | async-done | bytes 589840
  832.7 44.2 %reduce-scatter.21.cloned.1.call-done = bf16[3072,96]{0,1:T(8,128)(2,1)} async-done(((bf16[3072,768]{0,1:T(8,128)(2,1)}), bf16[3072,96]{0,1:T(8,128)(2,1)}) %reduce-scatter.21.cloned.1.call-update) | async-done | bytes 589840 | tf_op jit(solution)/shard_map/reduce_scatter | solution.py:328
  876.9 6.4 fusion.74
  883.3 40.4 %all-reduce = (f32[768]{0:T(1024)}, f32[768]{0:T(1024)}, f32[768]{0:T(1024)}, f32[768]{0:T(1024)}, f32[9]{0:T(128)}) all-reduce(f32[768]{0:T(1024)S(1)} %get-tuple-element.307, f32[768]{0:T(1024)S(1)} %get-tuple-element.312, f32[768]{0:T(1024)S(1)} %copy-done.36, ...), channel_id=1, replica_groups=mesh['batch'=4,'seq'=8] {'batch','seq'}, use_global_device_ids=true, to_apply=%region_25.28 | all-reduce | flops 3081 | bytes 24648 | tf_op jit(solution)/shard_map/psum | solution.py:346
  930.0 15.0 %reduce-scatter.19.cloned.1.call-done = bf16[192,384]{1,0:T(8,128)(2,1)} async-done(((bf16[768,384]{1,0:T(8,128)(2,1)}), bf16[192,384]{1,0:T(8,128)(2,1)}) %reduce-scatter.19.cloned.1.call-update) | async-done | bytes 147472 | tf_op jit(solution)/shard_map/reduce_scatter | solution.py:339
  946.6 21.2 %reduce-scatter.23.cloned.1.call-done = bf16[768,96]{0,1:T(8,128)(2,1)} async-done(((bf16[3072,96]{0,1:T(8,128)(2,1)}), bf16[768,96]{0,1:T(8,128)(2,1)}) %reduce-scatter.23.cloned.1.call-update) | async-done | bytes 147472 | tf_op jit(solution)/shard_map/reduce_scatter | solution.py:342
  (364 shorter events, 286.4 us)
Async XLA Ops:
  7.2 34.5 %copy-start.20 = (bf16[192,384]{1,0:T(8,128)(2,1)S(1)}, bf16[192,384]{1,0:T(8,128)(2,1)}, u32[]{:S(2)}) copy-start(bf16[192,384]{1,0:T(8,128)(2,1)} %param.27) | copy-start | bytes 442372
  7.2 51.6 %copy-start.53 = (s32[1,2]{1,0:T(1,128)S(1)}, s32[1,2]{1,0:T(1,128)}, u32[]{:S(2)}) copy-start(s32[1,2]{1,0:T(1,128)} %param.35) | copy-start | bytes 28
  7.2 51.7 %copy-start.44 = (s32[1,24]{1,0:T(1,128)S(1)}, s32[1,24]{1,0:T(1,128)}, u32[]{:S(2)}) copy-start(s32[1,24]{1,0:T(1,128)} %param.34) | copy-start | bytes 292
  7.2 51.8 %copy-start.3 = (bf16[512,768]{1,0:T(8,128)(2,1)S(1)}, bf16[512,768]{1,0:T(8,128)(2,1)}, u32[]{:S(2)}) copy-start(bf16[512,768]{1,0:T(8,128)(2,1)} %param.22) | copy-start | bytes 2359300
  7.2 55.3 %all-gather.5.cloned.1.call-start = ((), (), s32[]{:S(2)}) async-start(), calls=%async_computation.11 | async-start | bytes 3981312 | tf_op jit(solution)/shard_map/all_gather | solution.py:171
  26.9 35.7 %copy-start.38 = (f32[768]{0:T(1024)S(1)}, f32[768]{0:T(1024)}, u32[]{:S(2)}) copy-start(f32[768]{0:T(1024)} %param.29) | copy-start | bytes 9220
  26.9 35.7 %copy-start.49 = (f32[768]{0:T(1024)S(1)}, f32[768]{0:T(1024)}, u32[]{:S(2)}) copy-start(f32[768]{0:T(1024)} %param.30) | copy-start | bytes 9220
  26.9 268.1 %all-gather.7.cloned.1.call-start = ((), (), s32[]{:S(2)}) async-start(), calls=%async_computation.12 | async-start | bytes 1327104 | tf_op jit(solution)/shard_map/all_gather | solution.py:172
  41.6 256.2 %all-gather.9.cloned.1.call-start = ((), (), s32[]{:S(2)}) async-start(), calls=%async_computation.13 | async-start | bytes 5308416 | tf_op jit(solution)/shard_map/all_gather | solution.py:173
  59.2 7.5 copy-start.24
  62.5 14.6 %copy-start.15 = (f32[2,256,32]{1,0,2:T(2,128)}, f32[2,256,32]{1,0,2:T(2,128)S(1)}, u32[]{:S(2)}) copy-start(f32[2,256,32]{1,0,2:T(2,128)S(1)} %get-tuple-element.389) | copy-start | bytes 196612
  62.5 14.6 %copy-start.17 = (f32[2,256,32]{1,0,2:T(2,128)}, f32[2,256,32]{1,0,2:T(2,128)S(1)}, u32[]{:S(2)}) copy-start(f32[2,256,32]{1,0,2:T(2,128)S(1)} %get-tuple-element.390) | copy-start | bytes 196612
  62.5 36.9 %copy-start.33 = (s32[1024]{0:T(1024)}, s32[1024]{0:T(1024)S(1)}, u32[]{:S(2)}) copy-start(s32[1024]{0:T(1024)S(1)} %get-tuple-element.412) | copy-start | bytes 12292
  62.5 44.1 %copy-start.42 = (pred[24]{0:T(512)(128)(4,1)}, pred[24]{0:T(512)(128)(4,1)S(1)}, u32[]{:S(2)}) copy-start(pred[24]{0:T(512)(128)(4,1)S(1)} %compare_and_fusion.1) | copy-start | bytes 76
  112.1 49.9 %all-to-all-start = ((bf16[8,3,3,16384]{3,1,2,0:T(4,128)(2,1)}), bf16[8,3,3,16384]{3,1,2,0:T(4,128)(2,1)S(1)}, u32[]{:S(2)}, u32[]{:S(2)}) async-start(bf16[8,3,3,16384]{3,1,2,0:T(4,128)(2,1)} %copy.139), calls=%async_computation | async-start | bytes 6291456 | tf_op jit(solution)/shard_map/all_to_all | solution.py:186
  116.0 189.1 %all-gather.11.cloned.1.call-start = ((), (), s32[]{:S(2)}) async-start(), calls=%async_computation.14 | async-start | bytes 5308416 | tf_op jit(solution)/shard_map/all_gather | solution.py:174
  266.8 5.9 copy-start.22
  268.4 18.9 %all-to-all-start.1 = ((bf16[8,3,1,16384]{3,1,2,0:T(4,128)(2,1)}), bf16[8,3,1,16384]{3,1,2,0:T(4,128)(2,1)S(1)}, u32[]{:S(2)}, u32[]{:S(2)}) async-start(bf16[8,3,1,16384]{3,1,2,0:T(4,128)(2,1)} %copy.145), calls=%async_computation.1 | async-start | bytes 2097152 | tf_op jit(solution)/shard_map/all_to_all | solution.py:221
  272.7 16.3 %copy-start.32 = (s32[1024]{0:T(1024)}, s32[1024]{0:T(1024)S(1)}, u32[]{:S(2)}) copy-start(s32[1024]{0:T(1024)S(1)} %pad_clamp_fusion.1) | copy-start | bytes 12292
  273.4 15.6 %copy-start.40 = (pred[24]{0:T(512)(128)(4,1)}, pred[24]{0:T(512)(128)(4,1)S(1)}, u32[]{:S(2)}) copy-start(pred[24]{0:T(512)(128)(4,1)S(1)} %compare_and_fusion) | copy-start | bytes 76
  297.4 36.2 %copy-start.6 = (f32[512,768]{1,0:T(8,128)}, f32[512,768]{1,0:T(8,128)S(1)}, u32[]{:S(2)}) copy-start(f32[512,768]{1,0:T(8,128)S(1)} %get-tuple-element.405) | copy-start | bytes 4718596
  297.5 36.2 %copy-start.26 = (f32[512]{0:T(512)}, f32[512]{0:T(512)S(1)}, u32[]{:S(2)}) copy-start(f32[512]{0:T(512)S(1)} %broadcast_multiply_fusion.5) | copy-start | bytes 6148
  297.8 35.9 %copy-start.30 = (f32[512]{0:T(512)}, f32[512]{0:T(512)S(1)}, u32[]{:S(2)}) copy-start(f32[512]{0:T(512)S(1)} %add_rsqrt_fusion) | copy-start | bytes 6148
  297.8 7.4 copy-start.12
  305.2 10.1 %copy-start.46 = (bf16[768,3072]{1,0:T(8,128)(2,1)S(1)}, bf16[768,3072]{1,0:T(8,128)(2,1)}, u32[]{:S(2)}) copy-start(bf16[768,3072]{1,0:T(8,128)(2,1)} %all-gather.9.cloned.1.call-done) | copy-start | bytes 14155780
  318.8 14.9 %slice-start = ((s8[6291456]{0:T(1024)(128)(4,1)}), s8[4194304]{0:T(1024)(128)(4,1)S(1)}, s32[]{:S(2)}) async-start(s8[6291456]{0:T(1024)(128)(4,1)} %bitcast.284), calls=%async_computation.23 | async-start | bytes 8388608
  318.8 14.9 %slice-start.1 = ((s8[6291456]{0:T(1024)(128)(4,1)}), s8[2097152]{0:T(1024)(128)(4,1)S(1)}, s32[]{:S(2)}) async-start(s8[6291456]{0:T(1024)(128)(4,1)} %bitcast.284), calls=%async_computation.24 | async-start | bytes 4194304
  347.5 18.9 %all-to-all-start.2 = ((bf16[8,3,1,16384]{3,1,2,0:T(4,128)(2,1)}), bf16[8,3,1,16384]{3,1,2,0:T(4,128)(2,1)S(1)}, u32[]{:S(2)}, u32[]{:S(2)}) async-start(bf16[8,3,1,16384]{3,1,2,0:T(4,128)(2,1)} %bitcast.45), calls=%async_computation.2 | async-start | bytes 2097152 | tf_op jit(solution)/shard_map/all_to_all | solution.py:270
  351.1 388.7 %reduce-scatter.17.cloned.1.call-start = ((), (), s32[]{:S(2)}) async-start(), calls=%async_computation.16 | async-start | bytes 1327104 | tf_op jit(solution)/shard_map/reduce_scatter | solution.py:322
  355.5 406.9 %reduce-scatter.15.cloned.1.call-start = ((), (), s32[]{:S(2)}) async-start(), calls=%async_computation.15 | async-start | bytes 3981312 | tf_op jit(solution)/shard_map/reduce_scatter | solution.py:319
  636.1 4.9 collective-permute-start
  636.2 12.1 %collective-permute-start.1 = (bf16[1,3,3,16384]{3,2,1,0:T(4,128)(2,1)S(1)}, bf16[1,3,3,16384]{3,2,1,0:T(4,128)(2,1)S(1)}, u32[]{:S(2)}, u32[]{:S(2)}) collective-permute-start(bf16[1,3,3,16384]{3,2,1,0:T(4,128)(2,1)S(1)} %bitcast.310), channel_id=1, source_target_pairs={{0,2},{1,3},{2,0},{3,1},{4,6},{5,7},{6,4},{7,5},{8,10},{9,11},{10,... | collective-permute-start | bytes 884744 | tf_op jit(solution)/shard_map/ppermute | solution.py:130
  636.9 18.7 %collective-permute-start.2 = (bf16[1,3,3,16384]{3,2,1,0:T(4,128)(2,1)S(1)}, bf16[1,3,3,16384]{3,2,1,0:T(4,128)(2,1)S(1)}, u32[]{:S(2)}, u32[]{:S(2)}) collective-permute-start(bf16[1,3,3,16384]{3,2,1,0:T(4,128)(2,1)S(1)} %bitcast.307), channel_id=1, source_target_pairs={{0,3},{1,2},{2,1},{3,0},{4,7},{5,6},{6,5},{7,4},{8,11},{9,10},{10,... | collective-permute-start | bytes 884744 | tf_op jit(solution)/shard_map/ppermute | solution.py:130
  638.1 17.7 %collective-permute-start.3 = (bf16[1,3,3,16384]{3,2,1,0:T(4,128)(2,1)S(1)}, bf16[1,3,3,16384]{3,2,1,0:T(4,128)(2,1)S(1)}, u32[]{:S(2)}, u32[]{:S(2)}) collective-permute-start(bf16[1,3,3,16384]{3,2,1,0:T(4,128)(2,1)S(1)} %bitcast.306), channel_id=1, source_target_pairs={{0,4},{1,5},{2,6},{3,7},{4,0},{5,1},{6,2},{7,3},{8,12},{9,13},{10,... | collective-permute-start | bytes 884744 | tf_op jit(solution)/shard_map/ppermute | solution.py:130
  638.7 35.4 %collective-permute-start.4 = (bf16[1,3,3,16384]{3,2,1,0:T(4,128)(2,1)S(1)}, bf16[1,3,3,16384]{3,2,1,0:T(4,128)(2,1)S(1)}, u32[]{:S(2)}, u32[]{:S(2)}) collective-permute-start(bf16[1,3,3,16384]{3,2,1,0:T(4,128)(2,1)S(1)} %bitcast.305), channel_id=1, source_target_pairs={{0,5},{1,4},{2,7},{3,6},{4,1},{5,0},{6,3},{7,2},{8,13},{9,12},{10,... | collective-permute-start | bytes 884744 | tf_op jit(solution)/shard_map/ppermute | solution.py:130
  641.0 33.3 %collective-permute-start.5 = (bf16[1,3,3,16384]{3,2,1,0:T(4,128)(2,1)S(1)}, bf16[1,3,3,16384]{3,2,1,0:T(4,128)(2,1)S(1)}, u32[]{:S(2)}, u32[]{:S(2)}) collective-permute-start(bf16[1,3,3,16384]{3,2,1,0:T(4,128)(2,1)S(1)} %bitcast.309), channel_id=1, source_target_pairs={{0,6},{1,7},{2,4},{3,5},{4,2},{5,3},{6,0},{7,1},{8,14},{9,15},{10,... | collective-permute-start | bytes 884744 | tf_op jit(solution)/shard_map/ppermute | solution.py:130
  648.3 26.2 %collective-permute-start.6 = (bf16[1,3,3,16384]{3,2,1,0:T(4,128)(2,1)S(1)}, bf16[1,3,3,16384]{3,2,1,0:T(4,128)(2,1)S(1)}, u32[]{:S(2)}, u32[]{:S(2)}) collective-permute-start(bf16[1,3,3,16384]{3,2,1,0:T(4,128)(2,1)S(1)} %bitcast.308), channel_id=1, source_target_pairs={{0,7},{1,6},{2,5},{3,4},{4,3},{5,2},{6,1},{7,0},{8,15},{9,14},{10,... | collective-permute-start | bytes 884744 | tf_op jit(solution)/shard_map/ppermute | solution.py:130
  681.6 5.6 copy-start.41
  715.2 104.4 %reduce-scatter.29.cloned.1.call-start = ((), (), s32[]{:S(2)}) async-start(), calls=%async_computation.22 | async-start | bytes 5308416
  729.9 146.9 %reduce-scatter.21.cloned.1.call-start = ((), (), s32[]{:S(2)}) async-start(), calls=%async_computation.18 | async-start | bytes 5308416 | tf_op jit(solution)/shard_map/reduce_scatter | solution.py:328
  739.7 186.8 %reduce-scatter.27.cloned.1.call-start = ((), (), s32[]{:S(2)}) async-start(), calls=%async_computation.21 | async-start | bytes 245760
  741.5 186.6 %reduce-scatter.25.cloned.1.call-start = ((), (), s32[]{:S(2)}) async-start(), calls=%async_computation.20 | async-start | bytes 737280
  764.4 57.5 %copy-start.23 = (f32[9]{0:T(128)S(1)}, f32[9]{0:T(128)}, u32[]{:S(2)}) copy-start(f32[9]{0:T(128)} %param.33) | copy-start | bytes 112
  764.5 180.5 %reduce-scatter.19.cloned.1.call-start = ((), (), s32[]{:S(2)}) async-start(), calls=%async_computation.17 | async-start | bytes 737280 | tf_op jit(solution)/shard_map/reduce_scatter | solution.py:339
  821.8 146.1 %reduce-scatter.23.cloned.1.call-start = ((), (), s32[]{:S(2)}) async-start(), calls=%async_computation.19 | async-start | bytes 737280 | tf_op jit(solution)/shard_map/reduce_scatter | solution.py:342
  876.9 6.4 copy-start.36
  876.9 6.4 copy-start.37
  876.9 46.8 %copy-start.2 = (f32[512,768]{1,0:T(8,128)S(1)}, f32[512,768]{1,0:T(8,128)}, u32[]{:S(2)}) copy-start(f32[512,768]{1,0:T(8,128)} %copy-done.1) | copy-start | bytes 4718596
  (34 other events, 85.2 us)
Sparse Core Ops, SparseCore 0:
  27.0 35.0 all-gather.4
  64.5 23.9 all-gather.6
  90.4 47.8 all-gather.8
  140.0 55.4 all-gather.10
  355.6 37.7 reduce-scatter.16
  715.3 46.9 reduce-scatter.14
  765.8 53.7 reduce-scatter.28
  823.0 53.7 reduce-scatter.20
  879.7 19.5 reduce-scatter.26
  901.5 20.6 reduce-scatter.24
  924.4 20.5 reduce-scatter.18
  947.1 20.6 reduce-scatter.22
